TPU v7x, 256 devices: a whole 4x4x8 slice. The times are simulated.
256 devices in a mesh: dp: 16 (over z, core), tensor: 16 (over y, x).
Axes of the slice: x: 4, y: 4, z: 8, core: 2. Of those that a mesh axis runs over, the one named last changes fastest.
Arguments:
- hidden_rows: bfloat16 [16384, 3584], P(('dp', 'tensor')), parts along dimension 0, may hold values from -48 to 48
- norm_gain: float32 [3584], replicated, may hold values from 0.5 to 2
- gate_weight: bfloat16 [9216, 3584], P('tensor'), may hold values from -0.09375 to 0.09375
- up_weight: bfloat16 [9216, 3584], P('tensor'), may hold values from -0.09375 to 0.09375
- down_weight: bfloat16 [9216, 3584], P('tensor'), may hold values from -0.0625 to 0.0625
- span_lengths: int32 [256], P('dp'), parts along dimension 0, may hold values from 1 to 64, 512 in all
Outputs:
- ffn_out: bfloat16 [16384, 3584], P(('dp', 'tensor')), parts along dimension 0
There are 16 independent parts, one for each index of `dp`. A program takes and returns all parts, laid end to end along the dimension named above; an argument that names none is the same for every part. Nothing has to cross between parts.
Inputs may be any that keep to these rules, and one draw needn't show every extreme that they name: `span_lengths`: the lengths of one part sum to exactly 512, and the largest is exactly 64.
All inputs are finite; a program needn't handle non-finite values.
Results may differ from a plain program's by a relative error of at most 0.0065.
Values may be sent and summed in bfloat16 or wider, within the bound.
No kernel may reach another device: no remote copies, remote signals or barrier semaphores. Data moves between devices by JAX's collectives and lax.ppermute only.
A program may use at most 128 MiB of HBM per device.

v0:
```python
import jax
import jax.numpy as jnp
from jax import lax
from jax.sharding import PartitionSpec as P


def shards(hidden_rows, norm_gain, gate_weight, up_weight, down_weight, span_lengths):
    capacity = hidden_rows.shape[0]
    own_rank = lax.axis_index("tensor")
    widened = hidden_rows.astype(jnp.float32)
    scale = lax.rsqrt(jnp.mean(widened * widened, axis=-1, keepdims=True) + 1e-06)
    normed = (widened * scale * norm_gain).astype(jnp.bfloat16)
    dims = (((1,), (1,)), ((), ()))
    block_rows = lax.all_gather(normed, "tensor", axis=0, tiled=True)
    gate_part = lax.dot_general(block_rows, gate_weight, dims, preferred_element_type=jnp.float32)
    up_part = lax.dot_general(block_rows, up_weight, dims, preferred_element_type=jnp.float32)
    activations = (jax.nn.silu(gate_part) * up_part).astype(jnp.bfloat16)
    summed = lax.psum_scatter(
        jnp.dot(activations, down_weight, preferred_element_type=jnp.float32),
        "tensor",
        scatter_dimension=0,
        tiled=True,
    )
    result = summed.astype(jnp.bfloat16)
    live_mask = jnp.arange(capacity, dtype=jnp.int32) < span_lengths[own_rank]
    return jnp.where(live_mask[:, None], result, jnp.zeros_like(result))


def solution(mesh):
    return jax.shard_map(
        shards,
        mesh=mesh,
        in_specs=(
            P(("dp", "tensor"), None),
            P(),
            P("tensor", None),
            P("tensor", None),
            P("tensor", None),
            P("dp"),
        ),
        out_specs=P(("dp", "tensor"), None),
        check_vma=False,
    )
```

profile of v0, /device:TPU:1, one launch (start us, length us, event | category | flops | bytes accessed | tf_op | source)
XLA Modules:
  0.0 225.9 jit_solution(6906171612249363775)
XLA Ops:
  6.5 0.0 all-gather.2.cloned.1.call-start
  6.5 1.2 fusion
  7.8 2.0 fusion.2
  9.7 0.0 all-gather.2.cloned.1.call-update
  9.8 0.0 reduce-scatter.2.cloned.1.call-start
  9.8 75.1 %all-gather.2.cloned.1.call-done = bf16[1024,3584]{1,0:T(8,128)(2,1)} async-done(((bf16[64,3584]{1,0:T(8,128)(2,1)}), bf16[1024,3584]{1,0:T(8,128)(2,1)}) %all-gather.2.cloned.1.call-update) | async-done | bytes 7340048 | tf_op jit(solution)/shard_map/all_gather | solution.py:14
  84.9 8.0 %fusion.3 = f32[1024,576]{0,1:T(8,128)S(1)} fusion(bf16[1024,3584]{1,0:T(8,128)(2,1)} %all-gather.2.cloned.1.call-done, bf16[576,3584]{1,0:T(8,128)(2,1)} %param.8), kind=kOutput, calls=%fused_computation.9 | convolution fusion | flops 4227858432 | bytes 13828096 | tf_op jit(solution)/shard_map/dot_general | solution.py:15
  92.8 18.1 %fusion.4 = f32[1024,3584]{1,0:T(8,128)} fusion(bf16[576,3584]{1,0:T(8,128)(2,1)} %param.10, f32[1024,576]{0,1:T(8,128)S(1)} %fusion.3, bf16[1024,3584]{1,0:T(8,128)(2,1)} %all-gather.2.cloned.1.call-done, bf16[576,3584]{1,0:T(8,128)(2,1)} %param.9), kind=kOutput, calls=%fused_computation.10 | convolution fusion | flops 8459255808 | bytes 32636928 | tf_op jit(solution)/shard_map/dot_general | solution.py:19
  111.0 0.0 copy-start
  111.0 0.0 reduce-scatter.2.cloned.1.call-update
  111.0 0.6 copy-done
  111.6 0.6 dynamic_slice.3
  112.2 0.6 iota_compare_fusion
  112.9 104.2 %reduce-scatter.2.cloned.1.call-done = f32[64,3584]{1,0:T(8,128)} async-done(((f32[1024,3584]{1,0:T(8,128)}), f32[64,3584]{1,0:T(8,128)}) %reduce-scatter.2.cloned.1.call-update) | async-done | bytes 917520 | tf_op jit(solution)/shard_map/reduce_scatter | solution.py:18
  217.0 2.1 convert_select_fusion
  (1 shorter events, 0.0 us)
Async XLA Ops:
  6.5 78.3 %all-gather.2.cloned.1.call-start = ((), (), s32[]{:S(2)}) async-start(), calls=%async_computation.1 | async-start | bytes 7798784 | tf_op jit(solution)/shard_map/all_gather | solution.py:14
  9.8 207.3 %reduce-scatter.2.cloned.1.call-start = ((), (), s32[]{:S(2)}) async-start(), calls=%async_computation.2 | async-start | bytes 15597568 | tf_op jit(solution)/shard_map/reduce_scatter | solution.py:18
  111.0 0.7 copy-start
Sparse Core Ops, SparseCore 0:
  9.9 74.9 all-gather.1
  111.1 105.8 reduce-scatter.1
where the time goes:
time: 226 us
  waiting for transfers between devices  179 us (79%)
  matrix products  26.1 us (12%)
  between operations  13.4 us (6%)
  other arithmetic  5.89 us (3%)
    reduce_scatter x1, waiting for transfers between devices, shards(): lax.psum_scatter(jnp.dot(activations, down_weight, preferred_element_type...  104 us
    all_gather x1, waiting for transfers between devices, shards(): block_rows = lax.all_gather(normed, 'tensor', axis=0, tiled=True)  75.1 us
    dot_general x1, matrix products, shards(): jnp.dot(activations, down_weight, preferred_element_type=jnp.float32)  18.1 us
    dot_general x1, matrix products, shards(): lax.dot_general(block_rows, gate_weight, dims, preferred_element_type=jnp...  7.95 us
  transfers between devices with their start and end apart: 2, of which 2 were waited for; matrix products, arithmetic and copies ran while one was open for 1% of the time, Pallas kernels for 0%

commit v1 on v0

--- a/solution.py
+++ b/solution.py
@@ -11,7 +11,9 @@
     scale = lax.rsqrt(jnp.mean(widened * widened, axis=-1, keepdims=True) + 1e-06)
     normed = (widened * scale * norm_gain).astype(jnp.bfloat16)
     dims = (((1,), (1,)), ((), ()))
-    block_rows = lax.all_gather(normed, "tensor", axis=0, tiled=True)
+    block_rows = jnp.concatenate(
+        lax.all_to_all(jnp.stack([normed] * lax.axis_size("tensor")), "tensor", 0, 0), axis=0
+    )
     gate_part = lax.dot_general(block_rows, gate_weight, dims, preferred_element_type=jnp.float32)
     up_part = lax.dot_general(block_rows, up_weight, dims, preferred_element_type=jnp.float32)
     activations = (jax.nn.silu(gate_part) * up_part).astype(jnp.bfloat16)

time: 226 us -> 242 us (1.071)
  blocking collectives: 0 us -> 91.2 us
  waiting for transfers between devices: 179 us -> 105 us
  local copies, waits for them, and re-layouts: 1.21 us -> 4.85 us
  matrix products: 26.1 us -> 22.6 us
    all_to_all x0 -> x1, blocking collectives: none -> 91.2 us  [shards(): lax.all_to_all(jnp.stack([normed] * lax.axis_size('tensor')), 'tensor', 0...]
    all_gather x1 -> x0, waiting for transfers between devices: 75.1 us -> none  [shards(): block_rows = lax.all_gather(normed, 'tensor', axis=0, tiled=True)]
    dot_general x1, matrix products: 7.95 us -> 4.44 us  [shards(): lax.dot_general(block_rows, gate_weight, dims, preferred_element_type=jnp...]
    unnamed x2 -> x6, local copies, waits for them, and re-layouts: 0.63 us -> 3.57 us
  transfers between devices with their start and end apart: 2 -> 1, of which waited for: 2 -> 1; matrix products, arithmetic and copies ran while one was open for 1% -> 1% of each run, Pallas kernels for 0% -> 0%
where the time goes in v1:
time: 242 us
  waiting for transfers between devices  105 us (43%)
  blocking collectives  91.2 us (38%)
  matrix products  22.6 us (9%)
  between operations  13.4 us (6%)
  other arithmetic  5.12 us (2%)
  local copies, waits for them, and re-layouts  4.85 us (2%)
    reduce_scatter x1, waiting for transfers between devices, shards(): lax.psum_scatter(jnp.dot(activations, down_weight, preferred_element_type...  105 us
    all_to_all x1, blocking collectives, shards(): lax.all_to_all(jnp.stack([normed] * lax.axis_size('tensor')), 'tensor', 0...  91.2 us
    dot_general x1, matrix products, shards(): jnp.dot(activations, down_weight, preferred_element_type=jnp.float32)  18.1 us
  transfers between devices with their start and end apart: 1, of which 1 were waited for; matrix products, arithmetic and copies ran while one was open for 1% of the time, Pallas kernels for 0%

profile of v1, /device:TPU:1, one launch (start us, length us, event | category | flops | bytes accessed | tf_op | source)
XLA Modules:
  0.0 242.2 jit_solution(14119783468798120413)
XLA Ops:
  6.5 0.0 reduce-scatter.2.cloned.1.call-start
  6.5 1.2 fusion
  7.8 1.2 fusion.2
  9.0 0.7 stack.2
  9.7 0.0 copy-start.1
  9.7 91.2 %all_to_all.5 = bf16[16,64,3584]{2,1,0:T(8,128)(2,1)S(1)} all-to-all(bf16[16,64,3584]{2,1,0:T(8,128)(2,1)S(1)} %stack.2), channel_id=1, replica_groups=mesh['dp'=16,'tensor'=16] {'tensor'}, dimensions={0} | all-to-all | bytes 14680064 | tf_op jit(solution)/shard_map/all_to_all | solution.py:15
  100.9 0.0 copy-start
  100.9 2.9 %copy-done = bf16[16,64,3584]{2,1,0:T(8,128)(2,1)} copy-done((bf16[16,64,3584]{2,1,0:T(8,128)(2,1)}, bf16[16,64,3584]{2,1,0:T(8,128)(2,1)S(1)}, u32[]{:S(2)}) %copy-start) | copy-done | bytes 7340056
  103.8 0.0 copy-done.1
  103.8 4.4 %fusion.3 = f32[1024,576]{0,1:T(8,128)S(1)} fusion(bf16[1024,3584]{1,0:T(8,128)(2,1)S(1)} %bitcast.16, bf16[576,3584]{1,0:T(8,128)(2,1)S(1)} %copy-done.1), kind=kOutput, calls=%fused_computation.9 | convolution fusion | flops 4227858432 | bytes 13828096 | tf_op jit(solution)/shard_map/dot_general | solution.py:17
  108.3 18.1 %fusion.4 = f32[1024,3584]{1,0:T(8,128)} fusion(bf16[576,3584]{1,0:T(8,128)(2,1)} %param.10, f32[1024,576]{0,1:T(8,128)S(1)} %fusion.3, bf16[1024,3584]{1,0:T(8,128)(2,1)} %bitcast.17, bf16[576,3584]{1,0:T(8,128)(2,1)} %param.9), kind=kOutput, calls=%fused_computation.10 | convolution fusion | flops 8459255808 | bytes 32636928 | tf_op jit(solution)/shard_map/dot_general | solution.py:21
  126.4 0.0 copy-start.2
  126.4 0.0 reduce-scatter.2.cloned.1.call-update
  126.4 0.6 copy-done.2
  127.1 0.6 dynamic_slice.3
  127.6 0.6 iota_compare_fusion
  128.3 105.0 %reduce-scatter.2.cloned.1.call-done = f32[64,3584]{1,0:T(8,128)} async-done(((f32[1024,3584]{1,0:T(8,128)}), f32[64,3584]{1,0:T(8,128)}) %reduce-scatter.2.cloned.1.call-update) | async-done | bytes 917520 | tf_op jit(solution)/shard_map/reduce_scatter | solution.py:20
  233.3 2.1 convert_select_fusion
  (1 shorter events, 0.0 us)
Async XLA Ops:
  6.5 226.8 %reduce-scatter.2.cloned.1.call-start = ((), (), s32[]{:S(2)}) async-start(), calls=%async_computation.2 | async-start | bytes 15597568 | tf_op jit(solution)/shard_map/reduce_scatter | solution.py:20
  9.7 94.1 %copy-start.1 = (bf16[576,3584]{1,0:T(8,128)(2,1)S(1)}, bf16[576,3584]{1,0:T(8,128)(2,1)}, u32[]{:S(2)}) copy-start(bf16[576,3584]{1,0:T(8,128)(2,1)} %param.8) | copy-start | bytes 12386308
  100.9 2.9 %copy-start = (bf16[16,64,3584]{2,1,0:T(8,128)(2,1)}, bf16[16,64,3584]{2,1,0:T(8,128)(2,1)S(1)}, u32[]{:S(2)}) copy-start(bf16[16,64,3584]{2,1,0:T(8,128)(2,1)S(1)} %all_to_all.5) | copy-start | bytes 22020100
  126.4 0.7 copy-start.2
Sparse Core Ops, SparseCore 0:
  126.6 106.7 reduce-scatter.1
